TPU v7x, 32 devices: a whole 2x2x4 slice. The times are simulated.
32 devices in a mesh: node: 8 (over z, y), head: 4 (over x, core).
Axes of the slice: x: 2, y: 2, z: 4, core: 2. Of those that a mesh axis runs over, the one named last changes fastest.
Arguments:
- node_states: bfloat16 [3072, 1024], P('node'), may hold values from -12 to 12
- w_qkv: bfloat16 [1024, 3, 1024], P(None, None, 'head'), may hold values from -1 to 1
- w_out: bfloat16 [1024, 1024], P('head'), may hold values from -4 to 4
- ln_gain: float32 [1024], P('head'), may hold values from 0.5 to 1.5
- ln_bias: float32 [1024], P('head'), may hold values from -4 to 4
- local_mask: int32 [24, 7], P('node'), may hold values 0 or 1
- matchings: int32 [4, 24], P(None, 'node'), may hold values from 0 to 23, as said below
Outputs:
- layer_out: bfloat16 [3072, 1024], P('node', 'head')
Inputs may be any that keep to these rules, and one draw needn't show every extreme that they name: Each row of matchings is a perfect matching of the 24 blocks: matchings[m, matchings[m, b]] = b and matchings[m, b] differs from b. The blocks fall into groups of 3 consecutive blocks, and the number of groups is a power of two; for each m there is one number s_m, 1 <= s_m < 8, such that every block of group g is matched with a block of group g XOR s_m.
All inputs are finite; a program needn't handle non-finite values. No bound on the sum of `local_mask` on one device may be relied on, other than what follows from the above.
Results may differ from a plain program's by a relative error of at most 0.0077.
Values may be sent and summed in bfloat16 or wider, within the bound.
No kernel may reach another device: no remote copies, remote signals or barrier semaphores. Data moves between devices by JAX's collectives and lax.ppermute only.
A program may use at most 64 MiB of HBM per device.

v0:
```python
import math

import jax
import jax.numpy as jnp
from jax import lax
from jax.sharding import PartitionSpec as P

HEAD_DIM = 64
ROWS = 128
REACH = 3
GATHER_GROUPS = 16


NORM_EPS = 1e-05


def partner(array, axis, bit):
    return lax.ppermute(array, axis, [(i, i ^ 1 << bit) for i in range(lax.axis_size(axis))])


def with_halo(array, sides, width):
    for axis, dim in sides:
        devices, length = (lax.axis_size(axis), array.shape[dim])
        up = [(i, (i + 1) % devices) for i in range(devices - 1)]
        down = [(j, i) for i, j in up]
        last = lax.slice_in_dim(array, length - width, length, axis=dim)
        first = lax.slice_in_dim(array, 0, width, axis=dim)
        before = lax.ppermute(last, axis, up)
        after = lax.ppermute(first, axis, down)
        array = jnp.concatenate([before, array, after], axis=dim)
    return array


def shift_heads(array, step, devices):
    return lax.ppermute(array, "head", [(i, (i + step) % devices) for i in range(devices)])


def keep_same(current):
    return current


def route_direct(payload, shift_val, digits):
    for bit_pos in range(digits):

        def moved(current, bit_pos=bit_pos):
            return partner(current, "node", bit_pos)

        taken = jnp.bitwise_and(jnp.right_shift(shift_val, bit_pos), 1) == 1
        payload = lax.cond(taken, moved, keep_same, payload)
    return payload


def select_partner(received, matchings, blocks_here, pair_feats):
    matches = matchings.shape[0]
    received = received.reshape(matches, blocks_here, ROWS, pair_feats)
    sources = matchings % blocks_here
    selector = (sources[:, :, None] == jnp.arange(blocks_here)[None, None, :]).astype(jnp.bfloat16)
    picked = jnp.einsum("mjs,msrf->mjrf", selector, received, preferred_element_type=jnp.float32)
    return picked.astype(jnp.bfloat16)


def routed_keys(keyvals, matchings, my_index, groups, blocks_here, window):
    total_rows, pair_feats = keyvals.shape
    matches = matchings.shape[0]
    digits = groups.bit_length() - 1
    padded = with_halo(keyvals, (("node", 0),), REACH * ROWS)
    windows = jnp.stack(
        [padded[block_pos * ROWS : (block_pos + window) * ROWS] for block_pos in range(blocks_here)]
    )
    targets = jnp.bitwise_xor(matchings[:, 0] // blocks_here, my_index)
    received = jnp.stack(
        [route_direct(keyvals, targets[match_pos], digits) for match_pos in range(matches)]
    )
    partner_blocks = select_partner(received, matchings, blocks_here, pair_feats)
    partner_rows = jnp.transpose(partner_blocks, (1, 0, 2, 3)).reshape(
        blocks_here, matches * ROWS, pair_feats
    )
    return jnp.concatenate([windows, partner_rows], axis=1)


def switched_send(payload, shift_val, groups):
    def branch(shift):
        def moved(current):
            return lax.ppermute(current, "node", [(i, i ^ shift) for i in range(groups)])

        return moved

    branches = [branch(shift) for shift in range(1, groups)]
    return lax.switch(jnp.clip(shift_val - 1, 0, groups - 2), branches, payload)


def switched_keys(keyvals, matchings, my_index, groups, blocks_here, window):
    total_rows, pair_feats = keyvals.shape
    matches = matchings.shape[0]
    padded = with_halo(keyvals, (("node", 0),), REACH * ROWS)
    windows = jnp.stack(
        [padded[block_pos * ROWS : (block_pos + window) * ROWS] for block_pos in range(blocks_here)]
    )
    targets = jnp.bitwise_xor(matchings[:, 0] // blocks_here, my_index)
    picked = []
    for match_pos in range(matches):
        received = switched_send(keyvals, targets[match_pos], groups)
        received = received.reshape(blocks_here, ROWS, pair_feats)
        picked.append(jnp.take(received, matchings[match_pos] % blocks_here, axis=0, mode="clip"))
    partner_rows = jnp.stack(picked, axis=1).reshape(blocks_here, matches * ROWS, pair_feats)
    return jnp.concatenate([windows, partner_rows], axis=1)


def gathered_keys(keyvals, chosen):
    total_rows, pair_feats = keyvals.shape
    blocks_here, key_blocks = chosen.shape
    everyone = lax.all_gather(keyvals, "node", axis=0, tiled=True)
    everyone = everyone.reshape(-1, ROWS, pair_feats)
    picked = jnp.take(everyone, chosen.reshape(-1), axis=0, mode="clip")
    return picked.reshape(blocks_here, key_blocks * ROWS, pair_feats)


def local(node_states, w_qkv, w_out, ln_gain, ln_bias, local_mask, matchings):
    total_rows, model_width = node_states.shape
    blocks_here = total_rows // ROWS
    head_feats = w_qkv.shape[2]
    heads_here = head_feats // HEAD_DIM
    window = 2 * REACH + 1
    matches = matchings.shape[0]
    inv_root = 1.0 / math.sqrt(HEAD_DIM)
    my_index = lax.axis_index("node")
    groups = lax.axis_size("node")
    all_blocks = groups * blocks_here
    heads_axis = lax.axis_size("head")
    w_parts = [w_out] + [shift_heads(w_out, step, heads_axis) for step in range(1, heads_axis)]
    projected = jnp.einsum(
        "nd,dtf->ntf", node_states, w_qkv, preferred_element_type=jnp.float32
    ).astype(jnp.bfloat16)
    queries = projected[:, 0]
    keyvals = projected[:, 1:].reshape(total_rows, 2 * head_feats)
    global_blocks = my_index * blocks_here + jnp.arange(blocks_here, dtype=jnp.int32)
    offsets = jnp.arange(window, dtype=jnp.int32) - REACH
    neighbour = global_blocks[:, None] + offsets[None, :]
    if groups <= GATHER_GROUPS:
        key_rows = switched_keys(keyvals, matchings, my_index, groups, blocks_here, window)
    else:
        key_rows = routed_keys(keyvals, matchings, my_index, groups, blocks_here, window)
    key_count = key_rows.shape[1]
    key_part = key_rows[:, :, :head_feats].reshape(blocks_here, key_count, heads_here, HEAD_DIM)
    value_part = key_rows[:, :, head_feats:].reshape(blocks_here, key_count, heads_here, HEAD_DIM)
    query_blocks = queries.reshape(blocks_here, ROWS, heads_here, HEAD_DIM)
    local_ok = (
        (neighbour >= 0) & (neighbour < all_blocks) & ((offsets[None, :] == 0) | (local_mask == 1))
    )
    block_ok = jnp.concatenate([local_ok, jnp.ones((blocks_here, matches), dtype=bool)], axis=1)
    row_ok = jnp.repeat(block_ok, ROWS, axis=1)
    scores = (
        jnp.einsum("bqhd,bkhd->bhqk", query_blocks, key_part, preferred_element_type=jnp.float32)
        * inv_root
    )
    scores = jnp.where(row_ok[:, None, None, :], scores, -jnp.inf)
    highest = jnp.max(scores, axis=-1, keepdims=True)
    weights = jnp.exp(scores - highest)
    weights = (weights / jnp.sum(weights, axis=-1, keepdims=True)).astype(jnp.bfloat16)
    context = jnp.einsum("bhqk,bkhd->bqhd", weights, value_part, preferred_element_type=jnp.float32)
    context = context.astype(jnp.bfloat16).reshape(total_rows, head_feats)
    context_parts = [context] + [
        shift_heads(context, step, heads_axis) for step in range(1, heads_axis)
    ]
    mixed_rows = node_states.astype(jnp.float32) + jnp.einsum(
        "srf,sfo->ro",
        jnp.stack(context_parts),
        jnp.stack(w_parts),
        preferred_element_type=jnp.float32,
    )
    centre = jnp.mean(mixed_rows, axis=1, keepdims=True)
    deviation = mixed_rows - centre
    spread = jnp.mean(jnp.square(deviation), axis=1, keepdims=True)
    normed = deviation * lax.rsqrt(spread + NORM_EPS)
    out_cols = ln_gain.shape[0]
    col_start = lax.axis_index("head") * out_cols
    own_rows = lax.dynamic_slice_in_dim(normed, col_start, out_cols, 1)
    return (own_rows * ln_gain + ln_bias).astype(jnp.bfloat16)


def solution(mesh):
    placed = (
        P("node", None),
        P(None, None, "head"),
        P("head", None),
        P("head"),
        P("head"),
        P("node", None),
        P(None, "node"),
    )
    return jax.shard_map(
        local, mesh=mesh, in_specs=placed, out_specs=P("node", "head"), check_vma=False
    )
```

profile of v0, /device:TPU:9, one launch (start us, length us, event | category | flops | bytes accessed | tf_op | source)
XLA Modules:
  0.0 135.0 jit_solution(5089799291706525682)
XLA Ops:
  0.0 1.4 %copy-done = bf16[1024,3,256]{2,0,1:T(8,128)(2,1)S(1)} copy-done((bf16[1024,3,256]{2,0,1:T(8,128)(2,1)S(1)}, bf16[1024,3,256]{2,0,1:T(8,128)(2,1)}, u32[]{:S(2)}) %copy-start) | copy-done | bytes 1572888
  1.4 2.2 %convolution_convert_fusion = bf16[384,3,256]{0,2,1:T(8,128)(2,1)S(1)} fusion(bf16[1024,3,256]{2,0,1:T(8,128)(2,1)S(1)} %copy-done, bf16[384,1024]{1,0:T(8,128)(2,1)} %param.35), kind=kOutput, calls=%fused_computation.26 | convolution fusion | flops 604274688 | bytes 2949120 | tf_op jit(solution)/shard_map/nd,dtf->ntf/dot_general | solution.py:131
  3.6 3.1 %collective-permute-start.28 = (bf16[384,512]{0,1:T(8,128)(2,1)S(1)}, bf16[384,512]{0,1:T(8,128)(2,1)}, u32[]{:S(2)}, u32[]{:S(2)}) collective-permute-start(bf16[384,512]{0,1:T(8,128)(2,1)S(1)} %bitcast.87), channel_id=1, source_target_pairs={{0,4},{4,8},{8,12},{12,16},{16,20},{20,24},{24,28},{1,5},{5,9},{9,... | collective-permute-start | bytes 1179656 | tf_op jit(solution)/shard_map/ppermute | solution.py:28
  6.8 3.0 %collective-permute-start.29 = (bf16[384,512]{0,1:T(8,128)(2,1)S(1)}, bf16[384,512]{0,1:T(8,128)(2,1)}, u32[]{:S(2)}, u32[]{:S(2)}) collective-permute-start(bf16[384,512]{0,1:T(8,128)(2,1)S(1)} %bitcast.88), channel_id=1, source_target_pairs={{4,0},{8,4},{12,8},{16,12},{20,16},{24,20},{28,24},{5,1},{9,5},{13... | collective-permute-start | bytes 1179656 | tf_op jit(solution)/shard_map/ppermute | solution.py:29
  9.8 2.4 %collective-permute-start.33 = (bf16[256,1024]{1,0:T(8,128)(2,1)}, bf16[256,1024]{1,0:T(8,128)(2,1)}, u32[]{:S(2)}, u32[]{:S(2)}) collective-permute-start(bf16[256,1024]{1,0:T(8,128)(2,1)} %param.37), channel_id=1, source_target_pairs={{0,1},{1,2},{2,3},{3,0},{4,5},{5,6},{6,7},{7,4},{8,9},{9,10},{10,1... | collective-permute-start | bytes 1572872 | tf_op jit(solution)/shard_map/ppermute | solution.py:35
  12.2 0.3 collective-permute-start.34
  12.5 0.2 copy.39
  12.9 0.6 fusion.50
  14.8 20.0 %conditional.4 = (bf16[3,128,512]{2,1,0:T(8,128)(2,1)}) conditional(s32[]{:T(128)} %bitcast.33, bf16[384,512]{1,0:T(8,128)(2,1)S(1)} %copy.39, bf16[384,512]{1,0:T(8,128)(2,1)S(1)} %copy.39, bf16[384,512]{1,0:T(8,128)(2,1)S(1)} %copy.39, bf16[384,512]{1,0:T(8,128)(2,1)S(1)} %copy.39, ...), branch_computations={%region_0.1_spmd, %region_1.2_spmd, %region_2.3_spmd, %region_3.4_... | conditional | bytes 1572912 | solution.py:89
  14.9 1.4 %collective-permute-start.6 = (bf16[384,512]{1,0:T(8,128)(2,1)S(1)}, bf16[384,512]{1,0:T(8,128)(2,1)}, u32[]{:S(2)}, u32[]{:S(2)}) collective-permute-start(bf16[384,512]{1,0:T(8,128)(2,1)S(1)} %param.6), channel_id=1, source_target_pairs={{0,28},{4,24},{8,20},{12,16},{16,12},{20,8},{24,4},{28,0},{1,29},{... | collective-permute-start | bytes 1179656 | tf_op jit(solution)/shard_map/cond/branch_6_fun/ppermute | solution.py:84
  16.3 18.6 %collective-permute-done.6 = bf16[384,512]{1,0:T(8,128)(2,1)} collective-permute-done((bf16[384,512]{1,0:T(8,128)(2,1)S(1)}, bf16[384,512]{1,0:T(8,128)(2,1)}, u32[]{:S(2)}, u32[]{:S(2)}) %collective-permute-start.6) | collective-permute-done | bytes 393248 | tf_op jit(solution)/shard_map/cond/branch_6_fun/ppermute | solution.py:84
  34.9 10.6 %conditional.5 = (bf16[3,128,512]{2,1,0:T(8,128)(2,1)}) conditional(s32[]{:T(128)} %bitcast.37, bf16[384,512]{1,0:T(8,128)(2,1)S(1)} %copy.39, bf16[384,512]{1,0:T(8,128)(2,1)S(1)} %copy.39, bf16[384,512]{1,0:T(8,128)(2,1)S(1)} %copy.39, bf16[384,512]{1,0:T(8,128)(2,1)S(1)} %copy.39, ...), branch_computations={%region_7.8_spmd, %region_8.9_spmd, %region_9.10_spmd, %region_10.... | conditional | bytes 1572912 | solution.py:89
  34.9 10.6 %collective-permute-done.9 = bf16[384,512]{1,0:T(8,128)(2,1)} collective-permute-done((bf16[384,512]{1,0:T(8,128)(2,1)S(1)}, bf16[384,512]{1,0:T(8,128)(2,1)}, u32[]{:S(2)}, u32[]{:S(2)}) %collective-permute-start.9) | collective-permute-done | bytes 393248 | tf_op jit(solution)/shard_map/cond/branch_2_fun/ppermute | solution.py:84
  46.1 17.8 %conditional.6 = (bf16[3,128,512]{2,1,0:T(8,128)(2,1)}) conditional(s32[]{:T(128)} %bitcast.41, bf16[384,512]{1,0:T(8,128)(2,1)S(1)} %copy.39, bf16[384,512]{1,0:T(8,128)(2,1)S(1)} %copy.39, bf16[384,512]{1,0:T(8,128)(2,1)S(1)} %copy.39, bf16[384,512]{1,0:T(8,128)(2,1)S(1)} %copy.39, ...), branch_computations={%region_14.15_spmd, %region_15.16_spmd, %region_16.17_spmd, %regio... | conditional | bytes 1572912 | solution.py:89
  46.1 1.4 %collective-permute-start.17 = (bf16[384,512]{1,0:T(8,128)(2,1)S(1)}, bf16[384,512]{1,0:T(8,128)(2,1)}, u32[]{:S(2)}, u32[]{:S(2)}) collective-permute-start(bf16[384,512]{1,0:T(8,128)(2,1)S(1)} %param.17), channel_id=1, source_target_pairs={{0,16},{4,20},{8,24},{12,28},{16,0},{20,4},{24,8},{28,12},{1,17},{... | collective-permute-start | bytes 1179656 | tf_op jit(solution)/shard_map/cond/branch_3_fun/ppermute | solution.py:84
  47.5 16.4 %collective-permute-done.17 = bf16[384,512]{1,0:T(8,128)(2,1)} collective-permute-done((bf16[384,512]{1,0:T(8,128)(2,1)S(1)}, bf16[384,512]{1,0:T(8,128)(2,1)}, u32[]{:S(2)}, u32[]{:S(2)}) %collective-permute-start.17) | collective-permute-done | bytes 393248 | tf_op jit(solution)/shard_map/cond/branch_3_fun/ppermute | solution.py:84
  64.4 18.0 %conditional.7 = (bf16[3,128,512]{2,1,0:T(8,128)(2,1)}) conditional(s32[]{:T(128)} %bitcast.45, bf16[384,512]{1,0:T(8,128)(2,1)S(1)} %copy.39, bf16[384,512]{1,0:T(8,128)(2,1)S(1)} %copy.39, bf16[384,512]{1,0:T(8,128)(2,1)S(1)} %copy.39, bf16[384,512]{1,0:T(8,128)(2,1)S(1)} %copy.39, ...), branch_computations={%region_21.22_spmd, %region_22.23_spmd, %region_23.24_spmd, %regio... | conditional | bytes 1572912 | solution.py:89
  64.4 1.6 %collective-permute-start.26 = (bf16[384,512]{1,0:T(8,128)(2,1)S(1)}, bf16[384,512]{1,0:T(8,128)(2,1)}, u32[]{:S(2)}, u32[]{:S(2)}) collective-permute-start(bf16[384,512]{1,0:T(8,128)(2,1)S(1)} %param.26), channel_id=1, source_target_pairs={{0,24},{4,28},{8,16},{12,20},{16,8},{20,12},{24,0},{28,4},{1,25},{... | collective-permute-start | bytes 1179656 | tf_op jit(solution)/shard_map/cond/branch_5_fun/ppermute | solution.py:84
  66.0 16.4 %collective-permute-done.26 = bf16[384,512]{1,0:T(8,128)(2,1)} collective-permute-done((bf16[384,512]{1,0:T(8,128)(2,1)S(1)}, bf16[384,512]{1,0:T(8,128)(2,1)}, u32[]{:S(2)}, u32[]{:S(2)}) %collective-permute-start.26) | collective-permute-done | bytes 393248 | tf_op jit(solution)/shard_map/cond/branch_5_fun/ppermute | solution.py:84
  82.4 2.2 %collective-permute-start.35 = (bf16[256,1024]{1,0:T(8,128)(2,1)}, bf16[256,1024]{1,0:T(8,128)(2,1)}, u32[]{:S(2)}, u32[]{:S(2)}) collective-permute-start(bf16[256,1024]{1,0:T(8,128)(2,1)} %param.37), channel_id=1, source_target_pairs={{0,3},{1,0},{2,1},{3,2},{4,7},{5,4},{6,5},{7,6},{8,11},{9,8},{10,9... | collective-permute-start | bytes 1572872 | tf_op jit(solution)/shard_map/ppermute | solution.py:35
  84.7 0.7 slice.77
  85.4 2.3 %gather_fusion = bf16[3,128,512]{2,1,0:T(8,128)(2,1)} fusion(bf16[3,128,512]{2,1,0:T(8,128)(2,1)} %get-tuple-element.92, s32[1024]{0:T(1024)S(1)} %get-tuple-element.91), kind=kCustom, calls=%fused_computation | custom fusion | bytes 786444 | tf_op jit(solution)/shard_map/jit(_take)/gather | solution.py:104
  87.7 2.3 %gather_fusion.1 = bf16[3,128,512]{2,1,0:T(8,128)(2,1)} fusion(bf16[3,128,512]{2,1,0:T(8,128)(2,1)} %get-tuple-element.93, s32[1024]{0:T(1024)S(1)} %get-tuple-element.90), kind=kCustom, calls=%fused_computation.1 | custom fusion | bytes 786444 | tf_op jit(solution)/shard_map/jit(_take)/gather | solution.py:104
  90.1 2.3 %gather_fusion.2 = bf16[3,128,512]{2,1,0:T(8,128)(2,1)} fusion(bf16[3,128,512]{2,1,0:T(8,128)(2,1)} %get-tuple-element.94, s32[1024]{0:T(1024)S(1)} %get-tuple-element.89), kind=kCustom, calls=%fused_computation.2 | custom fusion | bytes 786444 | tf_op jit(solution)/shard_map/jit(_take)/gather | solution.py:104
  92.4 2.3 %gather_fusion.3 = bf16[3,128,512]{2,1,0:T(8,128)(2,1)} fusion(bf16[3,128,512]{2,1,0:T(8,128)(2,1)} %get-tuple-element.95, s32[1024]{0:T(1024)S(1)} %get-tuple-element.88), kind=kCustom, calls=%fused_computation.3 | custom fusion | bytes 786444 | tf_op jit(solution)/shard_map/jit(_take)/gather | solution.py:104
  94.7 1.5 %pad_maximum_fusion.1 = bf16[3,4,128,512]{3,2,1,0:T(8,128)(2,1)S(1)} fusion(bf16[3,1,128,512]{3,2,1,0:T(8,128)(2,1)} %bitcast.96, bf16[3,1,128,512]{3,2,1,0:T(8,128)(2,1)} %bitcast.95, bf16[3,1,128,512]{3,2,1,0:T(8,128)(2,1)} %bitcast.94, bf16[3,1,128,512]{3,2,1,0:T(8,128)(2,1)} %bitcast.93), kind=kLoop, calls=%fused_computation.23 | loop fusion | flops 2359296 | bytes 3145728 | tf_op jit(solution)/shard_map/stack | solution.py:105
  96.3 1.6 %copy.67 = bf16[3,512,512]{1,2,0:T(8,128)(2,1)} copy(bf16[3,512,512]{2,1,0:T(8,128)(2,1)S(1)} %bitcast.86) | data formatting | bytes 3145728 | tf_op jit(solution)/shard_map/reshape | solution.py:105
  98.0 1.0 reshape_squeeze.3
  99.1 1.2 pad_maximum_fusion.2
  100.3 0.2 slice_bitcast_fusion.2
  100.5 1.2 copy-done.1
  101.7 0.4 pad_maximum_fusion
  102.1 2.4 %fusion.49 = (bf16[3,1408,256]{1,2,0:T(8,128)(2,1)}, bf16[3,1408,256]{1,2,0:T(8,128)(2,1)}) fusion(bf16[3,1408,512]{1,2,0:T(8,128)(2,1)S(1)} %pad_maximum_fusion), kind=kLoop, calls=%fused_computation.82 | loop fusion | bytes 8650752 | tf_op jit(solution)/shard_map/slice | solution.py:144
  104.5 7.5 %fusion.51 = (f32[3,4,128]{2,1,0:T(4,128)S(1)}, f32[3,4,128,1408]{3,2,1,0:T(8,128)}) fusion(bf16[3,1408,4,64]{1,3,2,0:T(8,128)(2,1)} %bitcast.92, pred[3,1408]{1,0:T(4,128)(4,1)S(1)} %bitcast.97, bf16[3,128,4,64]{1,0,3,2:T(4,128)(2,1)S(1)} %reshape_squeeze.3), kind=kOutput, calls=%fused_computation.84 | convolution fusion | flops 285476224 | bytes 11020416 | tf_op jit(solution)/shard_map/sub | solution.py:158
  112.0 5.9 %fusion.19 = bf16[3,128,4,64]{1,3,2,0:T(8,128)(2,1)S(1)} fusion(bf16[3,1408,4,64]{1,3,2,0:T(8,128)(2,1)} %bitcast.91, f32[3,4,128,1408]{3,2,1,0:T(8,128)} %get-tuple-element.85, f32[3,4,128]{2,1,0:T(4,128)S(1)} %get-tuple-element.84), kind=kOutput, calls=%fused_computation.29 | convolution fusion | flops 281247744 | bytes 11016192 | tf_op jit(solution)/shard_map/bhqk,bkhd->bqhd/dot_general | solution.py:160
  118.0 0.3 copy.76
  118.2 0.3 reshape.410
  118.5 2.5 %collective-permute-start.30 = (bf16[384,256]{1,0:T(8,128)(2,1)S(1)}, bf16[384,256]{1,0:T(8,128)(2,1)S(1)}, u32[]{:S(2)}, u32[]{:S(2)}) collective-permute-start(bf16[384,256]{1,0:T(8,128)(2,1)S(1)} %reshape.410), channel_id=1, source_target_pairs={{0,1},{1,2},{2,3},{3,0},{4,5},{5,6},{6,7},{7,4},{8,9},{9,10},{10,1... | collective-permute-start | bytes 589832 | tf_op jit(solution)/shard_map/ppermute | solution.py:35
  121.1 0.3 collective-permute-start.31
  121.3 0.7 collective-permute-start.32
  122.0 0.3 reshape.409
  122.3 2.4 %collective-permute-done.30 = bf16[384,256]{1,0:T(8,128)(2,1)S(1)} collective-permute-done((bf16[384,256]{1,0:T(8,128)(2,1)S(1)}, bf16[384,256]{1,0:T(8,128)(2,1)S(1)}, u32[]{:S(2)}, u32[]{:S(2)}) %collective-permute-start.30) | collective-permute-done | bytes 196640 | tf_op jit(solution)/shard_map/ppermute | solution.py:35
  124.7 5.4 %collective-permute-done.31 = bf16[384,256]{1,0:T(8,128)(2,1)S(1)} collective-permute-done((bf16[384,256]{1,0:T(8,128)(2,1)S(1)}, bf16[384,256]{1,0:T(8,128)(2,1)S(1)}, u32[]{:S(2)}, u32[]{:S(2)}) %collective-permute-start.31) | collective-permute-done | bytes 196640 | tf_op jit(solution)/shard_map/ppermute | solution.py:35
  130.1 0.7 collective-permute-done.32
  130.8 2.7 %fusion.54 = (f32[384]{0:T(512)S(1)}, f32[384,1024]{1,0:T(8,128)S(1)}) fusion(bf16[1,256,1024]{2,1,0:T(8,128)(2,1)} %bitcast.59, bf16[1,256,1024]{2,1,0:T(8,128)(2,1)} %bitcast.58, bf16[1,256,1024]{2,1,0:T(8,128)(2,1)} %bitcast.57, bf16[1,256,1024]{2,1,0:T(8,128)(2,1)} %bitcast.56, bf16[1,384,256]{2,1,0:T(8,128)(2,1)} %bitcast.55, ...), kind=kOutput, calls=%fused_computation.85 | convolution fusion | flops 810811008 | bytes 5244416 | tf_op jit(solution)/shard_map/srf,sfo->ro/dot_general | solution.py:165
  133.5 0.3 multiply_reduce_fusion
  133.8 0.3 copy-done.4
  134.2 0.8 fusion.30
  (33 shorter events, 0.6 us)
Async XLA Ops:
  0.0 1.4 %copy-start = (bf16[1024,3,256]{2,0,1:T(8,128)(2,1)S(1)}, bf16[1024,3,256]{2,0,1:T(8,128)(2,1)}, u32[]{:S(2)}) copy-start(bf16[1024,3,256]{2,0,1:T(8,128)(2,1)} %param.36) | copy-start | bytes 4718596
  0.0 12.7 %copy-start.2 = (s32[4,3]{1,0:T(4,128)S(1)}, s32[4,3]{1,0:T(4,128)}, u32[]{:S(2)}) copy-start(s32[4,3]{1,0:T(4,128)} %param.41) | copy-start | bytes 148
  3.6 95.4 %collective-permute-start.28 = (bf16[384,512]{0,1:T(8,128)(2,1)S(1)}, bf16[384,512]{0,1:T(8,128)(2,1)}, u32[]{:S(2)}, u32[]{:S(2)}) collective-permute-start(bf16[384,512]{0,1:T(8,128)(2,1)S(1)} %bitcast.87), channel_id=1, source_target_pairs={{0,4},{4,8},{8,12},{12,16},{16,20},{20,24},{24,28},{1,5},{5,9},{9,... | collective-permute-start | bytes 1179656 | tf_op jit(solution)/shard_map/ppermute | solution.py:28
  6.8 92.3 %collective-permute-start.29 = (bf16[384,512]{0,1:T(8,128)(2,1)S(1)}, bf16[384,512]{0,1:T(8,128)(2,1)}, u32[]{:S(2)}, u32[]{:S(2)}) collective-permute-start(bf16[384,512]{0,1:T(8,128)(2,1)S(1)} %bitcast.88), channel_id=1, source_target_pairs={{4,0},{8,4},{12,8},{16,12},{20,16},{24,20},{28,24},{5,1},{9,5},{13... | collective-permute-start | bytes 1179656 | tf_op jit(solution)/shard_map/ppermute | solution.py:29
  9.8 111.5 %collective-permute-start.33 = (bf16[256,1024]{1,0:T(8,128)(2,1)}, bf16[256,1024]{1,0:T(8,128)(2,1)}, u32[]{:S(2)}, u32[]{:S(2)}) collective-permute-start(bf16[256,1024]{1,0:T(8,128)(2,1)} %param.37), channel_id=1, source_target_pairs={{0,1},{1,2},{2,3},{3,0},{4,5},{5,6},{6,7},{7,4},{8,9},{9,10},{10,1... | collective-permute-start | bytes 1572872 | tf_op jit(solution)/shard_map/ppermute | solution.py:35
  12.2 110.1 %collective-permute-start.34 = (bf16[256,1024]{1,0:T(8,128)(2,1)}, bf16[256,1024]{1,0:T(8,128)(2,1)}, u32[]{:S(2)}, u32[]{:S(2)}) collective-permute-start(bf16[256,1024]{1,0:T(8,128)(2,1)} %param.37), channel_id=1, source_target_pairs={{0,2},{1,3},{2,0},{3,1},{4,6},{5,7},{6,4},{7,5},{8,10},{9,11},{10,... | collective-permute-start | bytes 1572872 | tf_op jit(solution)/shard_map/ppermute | solution.py:35
  14.9 20.0 %collective-permute-start.6 = (bf16[384,512]{1,0:T(8,128)(2,1)S(1)}, bf16[384,512]{1,0:T(8,128)(2,1)}, u32[]{:S(2)}, u32[]{:S(2)}) collective-permute-start(bf16[384,512]{1,0:T(8,128)(2,1)S(1)} %param.6), channel_id=1, source_target_pairs={{0,28},{4,24},{8,20},{12,16},{16,12},{20,8},{24,4},{28,0},{1,29},{... | collective-permute-start | bytes 1179656 | tf_op jit(solution)/shard_map/cond/branch_6_fun/ppermute | solution.py:84
  34.9 10.6 %collective-permute-start.9 = (bf16[384,512]{1,0:T(8,128)(2,1)S(1)}, bf16[384,512]{1,0:T(8,128)(2,1)}, u32[]{:S(2)}, u32[]{:S(2)}) collective-permute-start(bf16[384,512]{1,0:T(8,128)(2,1)S(1)} %param.9), channel_id=1, source_target_pairs={{0,12},{4,8},{8,4},{12,0},{16,28},{20,24},{24,20},{28,16},{1,13},{... | collective-permute-start | bytes 1179656 | tf_op jit(solution)/shard_map/cond/branch_2_fun/ppermute | solution.py:84
  46.1 17.7 %collective-permute-start.17 = (bf16[384,512]{1,0:T(8,128)(2,1)S(1)}, bf16[384,512]{1,0:T(8,128)(2,1)}, u32[]{:S(2)}, u32[]{:S(2)}) collective-permute-start(bf16[384,512]{1,0:T(8,128)(2,1)S(1)} %param.17), channel_id=1, source_target_pairs={{0,16},{4,20},{8,24},{12,28},{16,0},{20,4},{24,8},{28,12},{1,17},{... | collective-permute-start | bytes 1179656 | tf_op jit(solution)/shard_map/cond/branch_3_fun/ppermute | solution.py:84
  64.4 18.0 %collective-permute-start.26 = (bf16[384,512]{1,0:T(8,128)(2,1)S(1)}, bf16[384,512]{1,0:T(8,128)(2,1)}, u32[]{:S(2)}, u32[]{:S(2)}) collective-permute-start(bf16[384,512]{1,0:T(8,128)(2,1)S(1)} %param.26), channel_id=1, source_target_pairs={{0,24},{4,28},{8,16},{12,20},{16,8},{20,12},{24,0},{28,4},{1,25},{... | collective-permute-start | bytes 1179656 | tf_op jit(solution)/shard_map/cond/branch_5_fun/ppermute | solution.py:84
  82.4 39.9 %collective-permute-start.35 = (bf16[256,1024]{1,0:T(8,128)(2,1)}, bf16[256,1024]{1,0:T(8,128)(2,1)}, u32[]{:S(2)}, u32[]{:S(2)}) collective-permute-start(bf16[256,1024]{1,0:T(8,128)(2,1)} %param.37), channel_id=1, source_target_pairs={{0,3},{1,0},{2,1},{3,2},{4,7},{5,4},{6,5},{7,6},{8,11},{9,8},{10,9... | collective-permute-start | bytes 1572872 | tf_op jit(solution)/shard_map/ppermute | solution.py:35
  96.3 1.6 %copy-start.3 = (s32[3,7]{1,0:T(4,128)S(1)}, s32[3,7]{1,0:T(4,128)}, u32[]{:S(2)}) copy-start(s32[3,7]{1,0:T(4,128)} %param.40) | copy-start | bytes 256
  100.3 1.4 %copy-start.1 = (bf16[3,512,512]{1,2,0:T(8,128)(2,1)S(1)}, bf16[3,512,512]{1,2,0:T(8,128)(2,1)}, u32[]{:S(2)}) copy-start(bf16[3,512,512]{1,2,0:T(8,128)(2,1)} %copy.67) | copy-start | bytes 4718596
  112.0 18.8 %copy-start.6 = (bf16[384,1024]{1,0:T(8,128)(2,1)S(1)}, bf16[384,1024]{1,0:T(8,128)(2,1)}, u32[]{:S(2)}) copy-start(bf16[384,1024]{1,0:T(8,128)(2,1)} %param.35) | copy-start | bytes 2359300
  118.5 6.2 %collective-permute-start.30 = (bf16[384,256]{1,0:T(8,128)(2,1)S(1)}, bf16[384,256]{1,0:T(8,128)(2,1)S(1)}, u32[]{:S(2)}, u32[]{:S(2)}) collective-permute-start(bf16[384,256]{1,0:T(8,128)(2,1)S(1)} %reshape.410), channel_id=1, source_target_pairs={{0,1},{1,2},{2,3},{3,0},{4,5},{5,6},{6,7},{7,4},{8,9},{9,10},{10,1... | collective-permute-start | bytes 589832 | tf_op jit(solution)/shard_map/ppermute | solution.py:35
  121.1 9.0 %collective-permute-start.31 = (bf16[384,256]{1,0:T(8,128)(2,1)S(1)}, bf16[384,256]{1,0:T(8,128)(2,1)S(1)}, u32[]{:S(2)}, u32[]{:S(2)}) collective-permute-start(bf16[384,256]{1,0:T(8,128)(2,1)S(1)} %reshape.410), channel_id=1, source_target_pairs={{0,2},{1,3},{2,0},{3,1},{4,6},{5,7},{6,4},{7,5},{8,10},{9,11},{10,... | collective-permute-start | bytes 589832 | tf_op jit(solution)/shard_map/ppermute | solution.py:35
  121.3 9.5 %collective-permute-start.32 = (bf16[384,256]{1,0:T(8,128)(2,1)S(1)}, bf16[384,256]{1,0:T(8,128)(2,1)}, u32[]{:S(2)}, u32[]{:S(2)}) collective-permute-start(bf16[384,256]{1,0:T(8,128)(2,1)S(1)} %reshape.410), channel_id=1, source_target_pairs={{0,3},{1,0},{2,1},{3,2},{4,7},{5,4},{6,5},{7,6},{8,11},{9,8},{10,9... | collective-permute-start | bytes 589832 | tf_op jit(solution)/shard_map/ppermute | solution.py:35
  133.5 0.7 copy-start.4
  133.5 0.7 copy-start.5
where the time goes:
time: 133 us; the launch traced here: 135 us
  waiting for transfers between devices  70.4 us (53%)
  local copies, waits for them, and re-layouts  19.9 us (15%)
  starting transfers between devices  18.9 us (14%)
  matrix products  18.3 us (14%)
  other arithmetic  4.65 us (3%)
  between operations  2.73 us (2%)
    ppermute x4, waiting for transfers between devices, moved(): lax.ppermute(current, 'node', [(i, i ^ shift) for i in range(groups)])  61.9 us
    gather x4, local copies, waits for them, and re-layouts, switched_keys(): jnp.take(received, matchings[match_pos] % blocks_here, axis=0, mode='clip')  9.33 us
    ppermute x6, waiting for transfers between devices, shift_heads(): lax.ppermute(array, 'head', [(i, (i + step) % devices) for i in range(dev...  8.53 us
    ppermute x6, starting transfers between devices, shift_heads(): lax.ppermute(array, 'head', [(i, (i + step) % devices) for i in range(dev...  8.33 us
    sub x1, matrix products, local(): weights = jnp.exp(scores - highest)  7.51 us
    dot_general x1, matrix products, local(): jnp.einsum('bhqk,bkhd->bqhd', weights, value_part, preferred_element_type...  5.95 us
    ppermute x4, starting transfers between devices, moved(): lax.ppermute(current, 'node', [(i, i ^ shift) for i in range(groups)])  4.41 us
    ppermute x1, starting transfers between devices, with_halo(): before = lax.ppermute(last, axis, up)  3.15 us
  transfers between devices with their start and end apart: 12, of which 7 were waited for; matrix products, arithmetic and copies ran while one was open for 25% of the time, Pallas kernels for 0%

commit v1 on v0

--- a/solution.py
+++ b/solution.py
@@ -101,6 +101,57 @@
     for match_pos in range(matches):
         received = switched_send(keyvals, targets[match_pos], groups)
         received = received.reshape(blocks_here, ROWS, pair_feats)
+        picked.append(jnp.take(received, matchings[match_pos] % blocks_here, axis=0, mode="clip"))
+    partner_rows = jnp.stack(picked, axis=1).reshape(blocks_here, matches * ROWS, pair_feats)
+    return jnp.concatenate([windows, partner_rows], axis=1)
+
+
+def spread_rows(pieces, heads_axis, me):
+    slots = {0: pieces}
+    for bit in reversed(range(heads_axis.bit_length() - 1)):
+        flip = 1 << bit
+        held = sorted(slots)
+        other = lax.ppermute(
+            jnp.stack([slots[k] for k in held]),
+            "head",
+            [(i, i ^ flip) for i in range(heads_axis)],
+        )
+        for pos, k in enumerate(held):
+            slots[k ^ flip] = other[pos]
+    count, part_rows, width = pieces.shape
+    rows = jnp.zeros((count, heads_axis * part_rows, width), pieces.dtype)
+    for k, part in slots.items():
+        rows = lax.dynamic_update_slice_in_dim(rows, part, (me ^ k) * part_rows, axis=1)
+    return rows
+
+
+def quarter_keys(node_states, w_qkv, keyvals, matchings, my_index, groups, blocks_here, window):
+    total_rows, pair_feats = keyvals.shape
+    matches = matchings.shape[0]
+    heads_axis = lax.axis_size("head")
+    part_rows = total_rows // heads_axis
+    me = lax.axis_index("head")
+    mine = lax.dynamic_slice_in_dim(node_states, me * part_rows, part_rows, 0)
+    up = [(i, i + 1) for i in range(groups - 1)]
+    down = [(i + 1, i) for i in range(groups - 1)]
+    before = lax.ppermute(mine, "node", up)
+    after = lax.ppermute(mine, "node", down)
+    targets = jnp.bitwise_xor(matchings[:, 0] // blocks_here, my_index)
+    matched = [switched_send(mine, targets[match_pos], groups) for match_pos in range(matches)]
+    rows = jnp.concatenate(
+        [spread_rows(piece[None], heads_axis, me) for piece in [before, after] + matched]
+    )
+    partner_kv = jnp.einsum(
+        "prd,dtf->prtf", rows, w_qkv[:, 1:], preferred_element_type=jnp.float32
+    ).astype(jnp.bfloat16)
+    partner_kv = partner_kv.reshape(rows.shape[0], total_rows, pair_feats)
+    padded = jnp.concatenate([partner_kv[0], keyvals, partner_kv[1]], axis=0)
+    windows = jnp.stack(
+        [padded[block_pos * ROWS : (block_pos + window) * ROWS] for block_pos in range(blocks_here)]
+    )
+    picked = []
+    for match_pos in range(matches):
+        received = partner_kv[2 + match_pos].reshape(blocks_here, ROWS, pair_feats)
         picked.append(jnp.take(received, matchings[match_pos] % blocks_here, axis=0, mode="clip"))
     partner_rows = jnp.stack(picked, axis=1).reshape(blocks_here, matches * ROWS, pair_feats)
     return jnp.concatenate([windows, partner_rows], axis=1)
@@ -137,7 +188,9 @@
     offsets = jnp.arange(window, dtype=jnp.int32) - REACH
     neighbour = global_blocks[:, None] + offsets[None, :]
     if groups <= GATHER_GROUPS:
-        key_rows = switched_keys(keyvals, matchings, my_index, groups, blocks_here, window)
+        key_rows = quarter_keys(
+            node_states, w_qkv, keyvals, matchings, my_index, groups, blocks_here, window
+        )
     else:
         key_rows = routed_keys(keyvals, matchings, my_index, groups, blocks_here, window)
     key_count = key_rows.shape[1]

time: 133 us -> 155 us (1.17)
  the two profiles are of different devices: /device:TPU:9 before, /device:TPU:1 now
where the time goes in v1:
time: 155 us
  starting transfers between devices  49.6 us (32%)
  waiting for transfers between devices  49.6 us (32%)
  matrix products  21.4 us (14%)
  local copies, waits for them, and re-layouts  20.8 us (13%)
  other arithmetic  9.85 us (6%)
  between operations  3.2 us (2%)
    ppermute x12, waiting for transfers between devices, spread_rows(): lax.ppermute(jnp.stack([slots[k] for k in held]), 'head', [(i, i ^ flip)...  23.8 us
    ppermute x12, starting transfers between devices, spread_rows(): lax.ppermute(jnp.stack([slots[k] for k in held]), 'head', [(i, i ^ flip)...  18.4 us
    ppermute x4, starting transfers between devices, moved(): lax.ppermute(current, 'node', [(i, i ^ shift) for i in range(groups)])  17 us
    ppermute x4, waiting for transfers between devices, moved(): lax.ppermute(current, 'node', [(i, i ^ shift) for i in range(groups)])  16.8 us
    ppermute x6, waiting for transfers between devices, shift_heads(): lax.ppermute(array, 'head', [(i, (i + step) % devices) for i in range(dev...  9.07 us
    ppermute x6, starting transfers between devices, shift_heads(): lax.ppermute(array, 'head', [(i, (i + step) % devices) for i in range(dev...  8.95 us
    sub x1, matrix products, local(): weights = jnp.exp(scores - highest)  7.51 us
    dot_general x1, matrix products, local(): jnp.einsum('bhqk,bkhd->bqhd', weights, value_part, preferred_element_type...  5.3 us
  transfers between devices with their start and end apart: 24, of which 15 were waited for; matrix products, arithmetic and copies ran while one was open for 29% of the time, Pallas kernels for 0%

profile of v1, /device:TPU:1, one launch (start us, length us, event | category | flops | bytes accessed | tf_op | source)
XLA Modules:
  0.0 154.6 jit_solution(17789248876894201182)
XLA Ops:
  0.0 1.6 %constant_dynamic-slice_fusion = bf16[96,1024]{1,0:T(8,128)(2,1)} fusion(bf16[384,1024]{1,0:T(8,128)(2,1)} %param.35, s32[]{:T(128)S(6)} %select_n.92), kind=kLoop, calls=%fused_computation.104 | loop fusion | bytes 393220 | tf_op jit(solution)/shard_map/dynamic_slice | solution.py:134
  1.6 4.0 %collective-permute-start.28 = (bf16[96,1024]{1,0:T(8,128)(2,1)}, bf16[96,1024]{1,0:T(8,128)(2,1)S(1)}, u32[]{:S(2)}, u32[]{:S(2)}) collective-permute-start(bf16[96,1024]{1,0:T(8,128)(2,1)} %constant_dynamic-slice_fusion), channel_id=1, source_target_pairs={{0,4},{4,8},{8,12},{12,16},{16,20},{20,24},{24,28},{1,5},{5,9},{9,... | collective-permute-start | bytes 589832 | tf_op jit(solution)/shard_map/ppermute | solution.py:137
  5.6 1.3 collective-permute-start.31
  9.8 9.6 %conditional.4 = (bf16[96,1024]{1,0:T(8,128)(2,1)}) conditional(s32[]{:T(128)} %bitcast.10, bf16[96,1024]{1,0:T(8,128)(2,1)} %constant_dynamic-slice_fusion, bf16[96,1024]{1,0:T(8,128)(2,1)} %constant_dynamic-slice_fusion, bf16[96,1024]{1,0:T(8,128)(2,1)} %constant_dynamic-slice_fusion, ...), branch_computations={%region_0.1_spmd, %region_1.2_spmd, %region_2.3_spmd, %region_3.4_... | conditional | bytes 786480 | solution.py:89
  9.8 5.2 %collective-permute-start.6 = (bf16[96,1024]{1,0:T(8,128)(2,1)}, bf16[96,1024]{1,0:T(8,128)(2,1)}, u32[]{:S(2)}, u32[]{:S(2)}) collective-permute-start(bf16[96,1024]{1,0:T(8,128)(2,1)} %param.6), channel_id=1, source_target_pairs={{0,28},{4,24},{8,20},{12,16},{16,12},{20,8},{24,4},{28,0},{1,29},{... | collective-permute-start | bytes 589832 | tf_op jit(solution)/shard_map/cond/branch_6_fun/ppermute | solution.py:84
  15.0 4.4 %collective-permute-done.6 = bf16[96,1024]{1,0:T(8,128)(2,1)} collective-permute-done((bf16[96,1024]{1,0:T(8,128)(2,1)}, bf16[96,1024]{1,0:T(8,128)(2,1)}, u32[]{:S(2)}, u32[]{:S(2)}) %collective-permute-start.6) | collective-permute-done | bytes 196640 | tf_op jit(solution)/shard_map/cond/branch_6_fun/ppermute | solution.py:84
  19.4 1.2 collective-permute-start.34
  21.3 9.1 %conditional.5 = (bf16[96,1024]{1,0:T(8,128)(2,1)}) conditional(s32[]{:T(128)} %bitcast.16, bf16[96,1024]{1,0:T(8,128)(2,1)} %constant_dynamic-slice_fusion, bf16[96,1024]{1,0:T(8,128)(2,1)} %constant_dynamic-slice_fusion, bf16[96,1024]{1,0:T(8,128)(2,1)} %constant_dynamic-slice_fusion, ...), branch_computations={%region_7.8_spmd, %region_8.9_spmd, %region_9.10_spmd, %region_10.... | conditional | bytes 786480 | solution.py:89
  21.3 5.7 %collective-permute-start.11 = (bf16[96,1024]{1,0:T(8,128)(2,1)}, bf16[96,1024]{1,0:T(8,128)(2,1)}, u32[]{:S(2)}, u32[]{:S(2)}) collective-permute-start(bf16[96,1024]{1,0:T(8,128)(2,1)} %param.11), channel_id=1, source_target_pairs={{0,20},{4,16},{8,28},{12,24},{16,4},{20,0},{24,12},{28,8},{1,21},{... | collective-permute-start | bytes 589832 | tf_op jit(solution)/shard_map/cond/branch_4_fun/ppermute | solution.py:84
  27.1 3.4 %collective-permute-done.11 = bf16[96,1024]{1,0:T(8,128)(2,1)} collective-permute-done((bf16[96,1024]{1,0:T(8,128)(2,1)}, bf16[96,1024]{1,0:T(8,128)(2,1)}, u32[]{:S(2)}, u32[]{:S(2)}) %collective-permute-start.11) | collective-permute-done | bytes 196640 | tf_op jit(solution)/shard_map/cond/branch_4_fun/ppermute | solution.py:84
  31.3 8.0 %conditional.6 = (bf16[96,1024]{1,0:T(8,128)(2,1)}) conditional(s32[]{:T(128)} %bitcast.22, bf16[96,1024]{1,0:T(8,128)(2,1)} %constant_dynamic-slice_fusion, bf16[96,1024]{1,0:T(8,128)(2,1)} %constant_dynamic-slice_fusion, bf16[96,1024]{1,0:T(8,128)(2,1)} %constant_dynamic-slice_fusion, ...), branch_computations={%region_14.15_spmd, %region_15.16_spmd, %region_16.17_spmd, %regio... | conditional | bytes 786480 | solution.py:89
  31.3 4.6 %collective-permute-start.16 = (bf16[96,1024]{1,0:T(8,128)(2,1)}, bf16[96,1024]{1,0:T(8,128)(2,1)}, u32[]{:S(2)}, u32[]{:S(2)}) collective-permute-start(bf16[96,1024]{1,0:T(8,128)(2,1)} %param.16), channel_id=1, source_target_pairs={{0,12},{4,8},{8,4},{12,0},{16,28},{20,24},{24,20},{28,16},{1,13},{... | collective-permute-start | bytes 589832 | tf_op jit(solution)/shard_map/cond/branch_2_fun/ppermute | solution.py:84
  35.9 3.4 %collective-permute-done.16 = bf16[96,1024]{1,0:T(8,128)(2,1)} collective-permute-done((bf16[96,1024]{1,0:T(8,128)(2,1)}, bf16[96,1024]{1,0:T(8,128)(2,1)}, u32[]{:S(2)}, u32[]{:S(2)}) %collective-permute-start.16) | collective-permute-done | bytes 196640 | tf_op jit(solution)/shard_map/cond/branch_2_fun/ppermute | solution.py:84
  39.9 7.0 %conditional.7 = (bf16[96,1024]{1,0:T(8,128)(2,1)}) conditional(s32[]{:T(128)} %bitcast.28, bf16[96,1024]{1,0:T(8,128)(2,1)} %constant_dynamic-slice_fusion, bf16[96,1024]{1,0:T(8,128)(2,1)} %constant_dynamic-slice_fusion, bf16[96,1024]{1,0:T(8,128)(2,1)} %constant_dynamic-slice_fusion, ...), branch_computations={%region_21.22_spmd, %region_22.23_spmd, %region_23.24_spmd, %regio... | conditional | bytes 786480 | solution.py:89
  39.9 1.4 collective-permute-start.21
  41.3 5.6 %collective-permute-done.21 = bf16[96,1024]{1,0:T(8,128)(2,1)} collective-permute-done((bf16[96,1024]{1,0:T(8,128)(2,1)}, bf16[96,1024]{1,0:T(8,128)(2,1)}, u32[]{:S(2)}, u32[]{:S(2)}) %collective-permute-start.21) | collective-permute-done | bytes 196640 | tf_op jit(solution)/shard_map/cond/branch_0_fun/ppermute | solution.py:84
  47.0 6.8 %collective-permute-start.45 = (bf16[256,1024]{1,0:T(8,128)(2,1)}, bf16[256,1024]{1,0:T(8,128)(2,1)}, u32[]{:S(2)}, u32[]{:S(2)}) collective-permute-start(bf16[256,1024]{1,0:T(8,128)(2,1)} %param.37), channel_id=1, source_target_pairs={{0,1},{1,2},{2,3},{3,0},{4,5},{5,6},{6,7},{7,4},{8,9},{9,10},{10,1... | collective-permute-start | bytes 1572872 | tf_op jit(solution)/shard_map/ppermute | solution.py:35
  53.7 0.8 fusion.61
  54.6 2.7 %convolution_convert_fusion = bf16[384,3,256]{0,2,1:T(8,128)(2,1)S(1)} fusion(bf16[1024,3,256]{2,0,1:T(8,128)(2,1)} %param.36, bf16[384,1024]{1,0:T(8,128)(2,1)} %param.35), kind=kOutput, calls=%fused_computation.29 | convolution fusion | flops 604274688 | bytes 2949120 | tf_op jit(solution)/shard_map/nd,dtf->ntf/dot_general | solution.py:182
  57.4 1.0 bitcast_dynamic-update-slice_fusion.7
  58.5 0.9 bitcast_dynamic-update-slice_fusion.5
  59.9 0.9 bitcast_dynamic-update-slice_fusion.3
  60.9 0.9 bitcast_dynamic-update-slice_fusion.1
  62.2 1.0 pad_maximum_fusion.5
  63.2 1.3 collective-permute-start.38
  64.5 1.0 pad_maximum_fusion.6
  65.5 13.9 %collective-permute-done.38 = bf16[1,1,96,1024]{3,2,1,0:T(8,128)(2,1)S(1)} collective-permute-done((bf16[1,1,96,1024]{3,2,1,0:T(8,128)(2,1)}, bf16[1,1,96,1024]{3,2,1,0:T(8,128)(2,1)S(1)}, u32[]{:S(2)}, u32[]{:S(2)}) %collective-permute-start.38) | collective-permute-done | bytes 196640 | tf_op jit(solution)/shard_map/ppermute | solution.py:114
  79.5 1.0 pad_maximum_fusion.7
  80.5 1.5 collective-permute-start.40
  82.4 5.0 %collective-permute-done.40 = bf16[1,1,96,1024]{3,2,1,0:T(8,128)(2,1)S(1)} collective-permute-done((bf16[1,1,96,1024]{3,2,1,0:T(8,128)(2,1)}, bf16[1,1,96,1024]{3,2,1,0:T(8,128)(2,1)S(1)}, u32[]{:S(2)}, u32[]{:S(2)}) %collective-permute-start.40) | collective-permute-done | bytes 196640 | tf_op jit(solution)/shard_map/ppermute | solution.py:114
  87.4 1.5 collective-permute-start.32
  88.9 1.0 pad_maximum_fusion.8
  89.9 1.7 %collective-permute-done.29 = bf16[1,1,96,1024]{3,2,1,0:T(8,128)(2,1)S(1)} collective-permute-done((bf16[1,1,96,1024]{3,2,1,0:T(8,128)(2,1)S(1)}, bf16[1,1,96,1024]{3,2,1,0:T(8,128)(2,1)S(1)}, u32[]{:S(2)}, u32[]{:S(2)}) %collective-permute-start.29) | collective-permute-done | bytes 196640 | tf_op jit(solution)/shard_map/ppermute | solution.py:114
  91.6 8.0 %collective-permute-start.35 = (bf16[2,1,96,1024]{3,2,1,0:T(8,128)(2,1)S(1)}, bf16[2,1,96,1024]{3,2,1,0:T(8,128)(2,1)S(1)}, u32[]{:S(2)}, u32[]{:S(2)}) collective-permute-start(bf16[2,1,96,1024]{3,2,1,0:T(8,128)(2,1)S(1)} %pad_maximum_fusion.5), channel_id=1, source_target_pairs={{0,1},{1,0},{2,3},{3,2},{4,5},{5,4},{6,7},{7,6},{8,9},{9,8},{10,11... | collective-permute-start | bytes 1179656 | tf_op jit(solution)/shard_map/ppermute | solution.py:114
  99.6 3.4 %collective-permute-start.37 = (bf16[2,1,96,1024]{3,2,1,0:T(8,128)(2,1)S(1)}, bf16[2,1,96,1024]{3,2,1,0:T(8,128)(2,1)S(1)}, u32[]{:S(2)}, u32[]{:S(2)}) collective-permute-start(bf16[2,1,96,1024]{3,2,1,0:T(8,128)(2,1)S(1)} %pad_maximum_fusion.6), channel_id=1, source_target_pairs={{0,1},{1,0},{2,3},{3,2},{4,5},{5,4},{6,7},{7,6},{8,9},{9,8},{10,11... | collective-permute-start | bytes 1179656 | tf_op jit(solution)/shard_map/ppermute | solution.py:114
  103.2 1.1 collective-permute-done.37
  106.8 1.1 collective-permute-done.33
  108.2 1.2 copy-done.5
  109.4 3.3 %fusion.18 = bf16[6,384,2,256]{1,3,2,0:T(8,128)(2,1)S(1)} fusion(bf16[6,384,1024]{2,1,0:T(8,128)(2,1)S(1)} %constant_dynamic-update-slice_fusion, bf16[1024,3,256]{2,0,1:T(8,128)(2,1)S(1)} %copy-done.5), kind=kOutput, calls=%fused_computation.25 | convolution fusion | flops 2417098752 | bytes 8126464 | tf_op jit(solution)/shard_map/prd,dtf->prtf/dot_general | solution.py:144
  113.8 1.6 %slice_bitcast_fusion.2 = (bf16[1,896,512]{1,2,0:T(8,128)(2,1)}, bf16[1,896,512]{1,2,0:T(8,128)(2,1)}, bf16[1,896,512]{1,2,0:T(8,128)(2,1)}) fusion(bf16[1152,512]{0,1:T(8,128)(2,1)S(1)} %pad_maximum_fusion.2), kind=kLoop, calls=%fused_computation.37 | loop fusion | bytes 5505024 | tf_op jit(solution)/shard_map/stack | solution.py:149
  122.3 1.9 %pad_maximum_fusion = bf16[3,1408,512]{1,2,0:T(8,128)(2,1)S(1)} fusion(bf16[3,512,512]{1,2,0:T(8,128)(2,1)S(1)} %copy.18, bf16[1,896,512]{1,2,0:T(8,128)(2,1)} %get-tuple-element.100, bf16[1,896,512]{1,2,0:T(8,128)(2,1)} %get-tuple-element.101, bf16[1,896,512]{1,2,0:T(8,128)(2,1)} %get-tuple-element.99), kind=kLoop, calls=%fused_computation.12 | loop fusion | flops 17301504 | bytes 8650752 | tf_op jit(solution)/shard_map/concatenate | solution.py:157
  124.3 1.7 %fusion.68 = (bf16[3,1408,256]{1,2,0:T(8,128)(2,1)}, bf16[3,1408,256]{1,2,0:T(8,128)(2,1)S(1)}) fusion(bf16[3,1408,512]{1,2,0:T(8,128)(2,1)S(1)} %pad_maximum_fusion), kind=kLoop, calls=%fused_computation.136 | loop fusion | bytes 8650752 | tf_op jit(solution)/shard_map/slice | solution.py:197
  125.9 7.5 %fusion.71 = (f32[3,4,128]{2,1,0:T(4,128)S(1)}, f32[3,4,128,1408]{3,2,1,0:T(8,128)}) fusion(bf16[3,1408,4,64]{1,3,2,0:T(8,128)(2,1)} %bitcast.151, pred[3,1408]{1,0:T(4,128)(4,1)S(1)} %bitcast.163, bf16[3,128,4,64]{1,0,3,2:T(4,128)(2,1)S(1)} %reshape_squeeze.19), kind=kOutput, calls=%fused_computation.139 | convolution fusion | flops 285476224 | bytes 11020416 | tf_op jit(solution)/shard_map/sub | solution.py:211
  133.4 5.3 %fusion.24 = bf16[3,128,4,64]{1,3,2,0:T(8,128)(2,1)S(1)} fusion(bf16[3,1408,4,64]{1,3,2,0:T(8,128)(2,1)S(1)} %bitcast.150, f32[3,4,128,1408]{3,2,1,0:T(8,128)} %get-tuple-element.111, f32[3,4,128]{2,1,0:T(4,128)S(1)} %get-tuple-element.110), kind=kOutput, calls=%fused_computation.32 | convolution fusion | flops 281247744 | bytes 11016192 | tf_op jit(solution)/shard_map/bhqk,bkhd->bqhd/dot_general | solution.py:213
  139.3 1.1 collective-permute-start.42
  141.4 3.1 %collective-permute-done.42 = bf16[384,256]{1,0:T(8,128)(2,1)S(1)} collective-permute-done((bf16[384,256]{1,0:T(8,128)(2,1)S(1)}, bf16[384,256]{1,0:T(8,128)(2,1)S(1)}, u32[]{:S(2)}, u32[]{:S(2)}) %collective-permute-start.42) | collective-permute-done | bytes 196640 | tf_op jit(solution)/shard_map/ppermute | solution.py:35
  144.5 5.3 %collective-permute-done.43 = bf16[384,256]{1,0:T(8,128)(2,1)S(1)} collective-permute-done((bf16[384,256]{1,0:T(8,128)(2,1)S(1)}, bf16[384,256]{1,0:T(8,128)(2,1)S(1)}, u32[]{:S(2)}, u32[]{:S(2)}) %collective-permute-start.43) | collective-permute-done | bytes 196640 | tf_op jit(solution)/shard_map/ppermute | solution.py:35
  150.4 2.6 %fusion.74 = (f32[384]{0:T(512)S(1)}, f32[384,1024]{1,0:T(8,128)S(1)}) fusion(bf16[1,256,1024]{2,1,0:T(8,128)(2,1)} %bitcast.66, bf16[1,256,1024]{2,1,0:T(8,128)(2,1)} %bitcast.65, bf16[1,256,1024]{2,1,0:T(8,128)(2,1)} %bitcast.64, bf16[1,256,1024]{2,1,0:T(8,128)(2,1)} %bitcast.63, bf16[1,384,256]{2,1,0:T(8,128)(2,1)S(1)} %bitcast.166, ...), kind=kOutput, calls=%fused_computation.140 | convolution fusion | flops 810811008 | bytes 5244416 | tf_op jit(solution)/shard_map/srf,sfo->ro/dot_general | solution.py:218
  (109 shorter events, 18.3 us)
Async XLA Ops:
  1.6 78.9 %collective-permute-start.28 = (bf16[96,1024]{1,0:T(8,128)(2,1)}, bf16[96,1024]{1,0:T(8,128)(2,1)S(1)}, u32[]{:S(2)}, u32[]{:S(2)}) collective-permute-start(bf16[96,1024]{1,0:T(8,128)(2,1)} %constant_dynamic-slice_fusion), channel_id=1, source_target_pairs={{0,4},{4,8},{8,12},{12,16},{16,20},{20,24},{24,28},{1,5},{5,9},{9,... | collective-permute-start | bytes 589832 | tf_op jit(solution)/shard_map/ppermute | solution.py:137
  5.6 76.6 %collective-permute-start.31 = (bf16[96,1024]{1,0:T(8,128)(2,1)}, bf16[96,1024]{1,0:T(8,128)(2,1)S(1)}, u32[]{:S(2)}, u32[]{:S(2)}) collective-permute-start(bf16[96,1024]{1,0:T(8,128)(2,1)} %constant_dynamic-slice_fusion), channel_id=1, source_target_pairs={{4,0},{8,4},{12,8},{16,12},{20,16},{24,20},{28,24},{5,1},{9,5},{13... | collective-permute-start | bytes 589832 | tf_op jit(solution)/shard_map/ppermute | solution.py:138
  9.8 9.6 %collective-permute-start.6 = (bf16[96,1024]{1,0:T(8,128)(2,1)}, bf16[96,1024]{1,0:T(8,128)(2,1)}, u32[]{:S(2)}, u32[]{:S(2)}) collective-permute-start(bf16[96,1024]{1,0:T(8,128)(2,1)} %param.6), channel_id=1, source_target_pairs={{0,28},{4,24},{8,20},{12,16},{16,12},{20,8},{24,4},{28,0},{1,29},{... | collective-permute-start | bytes 589832 | tf_op jit(solution)/shard_map/cond/branch_6_fun/ppermute | solution.py:84
  19.4 42.5 %collective-permute-start.34 = (bf16[1,1,96,1024]{3,2,1,0:T(8,128)(2,1)}, bf16[1,1,96,1024]{3,2,1,0:T(8,128)(2,1)S(1)}, u32[]{:S(2)}, u32[]{:S(2)}) collective-permute-start(bf16[1,1,96,1024]{3,2,1,0:T(8,128)(2,1)} %bitcast.12), channel_id=1, source_target_pairs={{0,2},{1,3},{2,0},{3,1},{4,6},{5,7},{6,4},{7,5},{8,10},{9,11},{10,... | collective-permute-start | bytes 589832 | tf_op jit(solution)/shard_map/ppermute | solution.py:114
  21.3 9.1 %collective-permute-start.11 = (bf16[96,1024]{1,0:T(8,128)(2,1)}, bf16[96,1024]{1,0:T(8,128)(2,1)}, u32[]{:S(2)}, u32[]{:S(2)}) collective-permute-start(bf16[96,1024]{1,0:T(8,128)(2,1)} %param.11), channel_id=1, source_target_pairs={{0,20},{4,16},{8,28},{12,24},{16,4},{20,0},{24,12},{28,8},{1,21},{... | collective-permute-start | bytes 589832 | tf_op jit(solution)/shard_map/cond/branch_4_fun/ppermute | solution.py:84
  30.4 32.8 %collective-permute-start.36 = (bf16[1,1,96,1024]{3,2,1,0:T(8,128)(2,1)}, bf16[1,1,96,1024]{3,2,1,0:T(8,128)(2,1)S(1)}, u32[]{:S(2)}, u32[]{:S(2)}) collective-permute-start(bf16[1,1,96,1024]{3,2,1,0:T(8,128)(2,1)} %bitcast.18), channel_id=1, source_target_pairs={{0,2},{1,3},{2,0},{3,1},{4,6},{5,7},{6,4},{7,5},{8,10},{9,11},{10,... | collective-permute-start | bytes 589832 | tf_op jit(solution)/shard_map/ppermute | solution.py:114
  31.3 8.0 %collective-permute-start.16 = (bf16[96,1024]{1,0:T(8,128)(2,1)}, bf16[96,1024]{1,0:T(8,128)(2,1)}, u32[]{:S(2)}, u32[]{:S(2)}) collective-permute-start(bf16[96,1024]{1,0:T(8,128)(2,1)} %param.16), channel_id=1, source_target_pairs={{0,12},{4,8},{8,4},{12,0},{16,28},{20,24},{24,20},{28,16},{1,13},{... | collective-permute-start | bytes 589832 | tf_op jit(solution)/shard_map/cond/branch_2_fun/ppermute | solution.py:84
  39.9 7.0 %collective-permute-start.21 = (bf16[96,1024]{1,0:T(8,128)(2,1)}, bf16[96,1024]{1,0:T(8,128)(2,1)}, u32[]{:S(2)}, u32[]{:S(2)}) collective-permute-start(bf16[96,1024]{1,0:T(8,128)(2,1)} %param.21), channel_id=1, source_target_pairs={{0,4},{4,0},{8,12},{12,8},{16,20},{20,16},{24,28},{28,24},{1,5},{5... | collective-permute-start | bytes 589832 | tf_op jit(solution)/shard_map/cond/branch_0_fun/ppermute | solution.py:84
  47.0 94.1 %collective-permute-start.45 = (bf16[256,1024]{1,0:T(8,128)(2,1)}, bf16[256,1024]{1,0:T(8,128)(2,1)}, u32[]{:S(2)}, u32[]{:S(2)}) collective-permute-start(bf16[256,1024]{1,0:T(8,128)(2,1)} %param.37), channel_id=1, source_target_pairs={{0,1},{1,2},{2,3},{3,0},{4,5},{5,6},{6,7},{7,4},{8,9},{9,10},{10,1... | collective-permute-start | bytes 1572872 | tf_op jit(solution)/shard_map/ppermute | solution.py:35
  57.3 2.6 %copy-start = (bf16[384,3,256]{0,2,1:T(8,128)(2,1)}, bf16[384,3,256]{0,2,1:T(8,128)(2,1)S(1)}, u32[]{:S(2)}) copy-start(bf16[384,3,256]{0,2,1:T(8,128)(2,1)S(1)} %convolution_convert_fusion) | copy-start | bytes 1769476
  57.3 2.2 %copy-start.2 = (s32[3,7]{1,0:T(4,128)S(1)}, s32[3,7]{1,0:T(4,128)}, u32[]{:S(2)}) copy-start(s32[3,7]{1,0:T(4,128)} %param.40) | copy-start | bytes 256
  61.9 79.4 %collective-permute-start.46 = (bf16[256,1024]{1,0:T(8,128)(2,1)}, bf16[256,1024]{1,0:T(8,128)(2,1)}, u32[]{:S(2)}, u32[]{:S(2)}) collective-permute-start(bf16[256,1024]{1,0:T(8,128)(2,1)} %param.37), channel_id=1, source_target_pairs={{0,2},{1,3},{2,0},{3,1},{4,6},{5,7},{6,4},{7,5},{8,10},{9,11},{10,... | collective-permute-start | bytes 1572872 | tf_op jit(solution)/shard_map/ppermute | solution.py:35
  63.2 16.2 %collective-permute-start.38 = (bf16[1,1,96,1024]{3,2,1,0:T(8,128)(2,1)}, bf16[1,1,96,1024]{3,2,1,0:T(8,128)(2,1)S(1)}, u32[]{:S(2)}, u32[]{:S(2)}) collective-permute-start(bf16[1,1,96,1024]{3,2,1,0:T(8,128)(2,1)} %bitcast.24), channel_id=1, source_target_pairs={{0,2},{1,3},{2,0},{3,1},{4,6},{5,7},{6,4},{7,5},{8,10},{9,11},{10,... | collective-permute-start | bytes 589832 | tf_op jit(solution)/shard_map/ppermute | solution.py:114
  79.4 62.0 %collective-permute-start.47 = (bf16[256,1024]{1,0:T(8,128)(2,1)}, bf16[256,1024]{1,0:T(8,128)(2,1)}, u32[]{:S(2)}, u32[]{:S(2)}) collective-permute-start(bf16[256,1024]{1,0:T(8,128)(2,1)} %param.37), channel_id=1, source_target_pairs={{0,3},{1,0},{2,1},{3,2},{4,7},{5,4},{6,5},{7,6},{8,11},{9,8},{10,9... | collective-permute-start | bytes 1572872 | tf_op jit(solution)/shard_map/ppermute | solution.py:35
  80.5 6.9 %collective-permute-start.40 = (bf16[1,1,96,1024]{3,2,1,0:T(8,128)(2,1)}, bf16[1,1,96,1024]{3,2,1,0:T(8,128)(2,1)S(1)}, u32[]{:S(2)}, u32[]{:S(2)}) collective-permute-start(bf16[1,1,96,1024]{3,2,1,0:T(8,128)(2,1)} %bitcast.30), channel_id=1, source_target_pairs={{0,2},{1,3},{2,0},{3,1},{4,6},{5,7},{6,4},{7,5},{8,10},{9,11},{10,... | collective-permute-start | bytes 589832 | tf_op jit(solution)/shard_map/ppermute | solution.py:114
  82.2 9.4 %collective-permute-start.29 = (bf16[1,1,96,1024]{3,2,1,0:T(8,128)(2,1)S(1)}, bf16[1,1,96,1024]{3,2,1,0:T(8,128)(2,1)S(1)}, u32[]{:S(2)}, u32[]{:S(2)}) collective-permute-start(bf16[1,1,96,1024]{3,2,1,0:T(8,128)(2,1)S(1)} %bitcast.161), channel_id=1, source_target_pairs={{0,2},{1,3},{2,0},{3,1},{4,6},{5,7},{6,4},{7,5},{8,10},{9,11},{10,... | collective-permute-start | bytes 589832 | tf_op jit(solution)/shard_map/ppermute | solution.py:114
  87.4 12.2 %collective-permute-start.32 = (bf16[1,1,96,1024]{3,2,1,0:T(8,128)(2,1)S(1)}, bf16[1,1,96,1024]{3,2,1,0:T(8,128)(2,1)S(1)}, u32[]{:S(2)}, u32[]{:S(2)}) collective-permute-start(bf16[1,1,96,1024]{3,2,1,0:T(8,128)(2,1)S(1)} %bitcast.159), channel_id=1, source_target_pairs={{0,2},{1,3},{2,0},{3,1},{4,6},{5,7},{6,4},{7,5},{8,10},{9,11},{10,... | collective-permute-start | bytes 589832 | tf_op jit(solution)/shard_map/ppermute | solution.py:114
  91.6 11.5 %collective-permute-start.35 = (bf16[2,1,96,1024]{3,2,1,0:T(8,128)(2,1)S(1)}, bf16[2,1,96,1024]{3,2,1,0:T(8,128)(2,1)S(1)}, u32[]{:S(2)}, u32[]{:S(2)}) collective-permute-start(bf16[2,1,96,1024]{3,2,1,0:T(8,128)(2,1)S(1)} %pad_maximum_fusion.5), channel_id=1, source_target_pairs={{0,1},{1,0},{2,3},{3,2},{4,5},{5,4},{6,7},{7,6},{8,9},{9,8},{10,11... | collective-permute-start | bytes 1179656 | tf_op jit(solution)/shard_map/ppermute | solution.py:114
  99.6 4.7 %collective-permute-start.37 = (bf16[2,1,96,1024]{3,2,1,0:T(8,128)(2,1)S(1)}, bf16[2,1,96,1024]{3,2,1,0:T(8,128)(2,1)S(1)}, u32[]{:S(2)}, u32[]{:S(2)}) collective-permute-start(bf16[2,1,96,1024]{3,2,1,0:T(8,128)(2,1)S(1)} %pad_maximum_fusion.6), channel_id=1, source_target_pairs={{0,1},{1,0},{2,3},{3,2},{4,5},{5,4},{6,7},{7,6},{8,9},{9,8},{10,11... | collective-permute-start | bytes 1179656 | tf_op jit(solution)/shard_map/ppermute | solution.py:114
  103.1 1.8 %collective-permute-start.39 = (bf16[2,1,96,1024]{3,2,1,0:T(8,128)(2,1)S(1)}, bf16[2,1,96,1024]{3,2,1,0:T(8,128)(2,1)S(1)}, u32[]{:S(2)}, u32[]{:S(2)}) collective-permute-start(bf16[2,1,96,1024]{3,2,1,0:T(8,128)(2,1)S(1)} %pad_maximum_fusion.7), channel_id=1, source_target_pairs={{0,1},{1,0},{2,3},{3,2},{4,5},{5,4},{6,7},{7,6},{8,9},{9,8},{10,11... | collective-permute-start | bytes 1179656 | tf_op jit(solution)/shard_map/ppermute | solution.py:114
  104.4 1.7 %collective-permute-start.41 = (bf16[2,1,96,1024]{3,2,1,0:T(8,128)(2,1)S(1)}, bf16[2,1,96,1024]{3,2,1,0:T(8,128)(2,1)S(1)}, u32[]{:S(2)}, u32[]{:S(2)}) collective-permute-start(bf16[2,1,96,1024]{3,2,1,0:T(8,128)(2,1)S(1)} %pad_maximum_fusion.8), channel_id=1, source_target_pairs={{0,1},{1,0},{2,3},{3,2},{4,5},{5,4},{6,7},{7,6},{8,9},{9,8},{10,11... | collective-permute-start | bytes 1179656 | tf_op jit(solution)/shard_map/ppermute | solution.py:114
  104.9 1.7 %collective-permute-start.30 = (bf16[2,1,96,1024]{3,2,1,0:T(8,128)(2,1)S(1)}, bf16[2,1,96,1024]{3,2,1,0:T(8,128)(2,1)S(1)}, u32[]{:S(2)}, u32[]{:S(2)}) collective-permute-start(bf16[2,1,96,1024]{3,2,1,0:T(8,128)(2,1)S(1)} %pad_maximum_fusion.3), channel_id=1, source_target_pairs={{0,1},{1,0},{2,3},{3,2},{4,5},{5,4},{6,7},{7,6},{8,9},{9,8},{10,11... | collective-permute-start | bytes 1179656 | tf_op jit(solution)/shard_map/ppermute | solution.py:114
  106.1 1.7 %collective-permute-start.33 = (bf16[2,1,96,1024]{3,2,1,0:T(8,128)(2,1)S(1)}, bf16[2,1,96,1024]{3,2,1,0:T(8,128)(2,1)S(1)}, u32[]{:S(2)}, u32[]{:S(2)}) collective-permute-start(bf16[2,1,96,1024]{3,2,1,0:T(8,128)(2,1)S(1)} %pad_maximum_fusion.4), channel_id=1, source_target_pairs={{0,1},{1,0},{2,3},{3,2},{4,5},{5,4},{6,7},{7,6},{8,9},{9,8},{10,11... | collective-permute-start | bytes 1179656 | tf_op jit(solution)/shard_map/ppermute | solution.py:114
  108.0 1.4 copy-start.5
  112.7 1.0 slice-start
  133.4 17.0 %copy-start.1 = (bf16[384,1024]{1,0:T(8,128)(2,1)S(1)}, bf16[384,1024]{1,0:T(8,128)(2,1)}, u32[]{:S(2)}) copy-start(bf16[384,1024]{1,0:T(8,128)(2,1)} %param.35) | copy-start | bytes 2359300
  139.3 5.2 %collective-permute-start.42 = (bf16[384,256]{1,0:T(8,128)(2,1)S(1)}, bf16[384,256]{1,0:T(8,128)(2,1)S(1)}, u32[]{:S(2)}, u32[]{:S(2)}) collective-permute-start(bf16[384,256]{1,0:T(8,128)(2,1)S(1)} %reshape.253), channel_id=1, source_target_pairs={{0,1},{1,2},{2,3},{3,0},{4,5},{5,6},{6,7},{7,4},{8,9},{9,10},{10,1... | collective-permute-start | bytes 589832 | tf_op jit(solution)/shard_map/ppermute | solution.py:35
  140.4 9.3 %collective-permute-start.43 = (bf16[384,256]{1,0:T(8,128)(2,1)S(1)}, bf16[384,256]{1,0:T(8,128)(2,1)S(1)}, u32[]{:S(2)}, u32[]{:S(2)}) collective-permute-start(bf16[384,256]{1,0:T(8,128)(2,1)S(1)} %reshape.253), channel_id=1, source_target_pairs={{0,2},{1,3},{2,0},{3,1},{4,6},{5,7},{6,4},{7,5},{8,10},{9,11},{10,... | collective-permute-start | bytes 589832 | tf_op jit(solution)/shard_map/ppermute | solution.py:35
  141.1 9.4 %collective-permute-start.44 = (bf16[384,256]{1,0:T(8,128)(2,1)S(1)}, bf16[384,256]{1,0:T(8,128)(2,1)S(1)}, u32[]{:S(2)}, u32[]{:S(2)}) collective-permute-start(bf16[384,256]{1,0:T(8,128)(2,1)S(1)} %reshape.253), channel_id=1, source_target_pairs={{0,3},{1,0},{2,1},{3,2},{4,7},{5,4},{6,5},{7,6},{8,11},{9,8},{10,9... | collective-permute-start | bytes 589832 | tf_op jit(solution)/shard_map/ppermute | solution.py:35
  153.1 0.7 copy-start.3
  153.1 0.7 copy-start.4
